TPU v7x, 32 devices: a whole 2x2x4 slice. The times are simulated.
32 devices in a mesh: dp: 4 (over y, x), seq: 8 (over z, core).
Axes of the slice: x: 2, y: 2, z: 4, core: 2. Of those that a mesh axis runs over, the one named last changes fastest.
Arguments:
- queries: bfloat16 [4, 8, 512, 2048], P('dp', 'seq'), may hold values from -48 to 48
- keys: bfloat16 [4, 8, 512, 2048], P('dp', 'seq'), may hold values from -6 to 6
- values: bfloat16 [4, 8, 512, 2048], P('dp', 'seq'), may hold values from -6 to 6
- out_grad: bfloat16 [4, 8, 512, 2048], P('dp', 'seq'), may hold values from -6 to 6
- out_weight: bfloat16 [2048, 2048], P('dp'), may hold values from -0.125 to 0.125
- row_mask: int32 [4, 4], replicated, may hold values from 0 to 1, as said below
- col_mask: int32 [8, 8], replicated, may hold values from 0 to 1, as said below
Outputs:
- layer_out: bfloat16 [4, 8, 512, 2048], P('dp', 'seq')
- query_grad: bfloat16 [4, 8, 512, 2048], P('dp', 'seq')
- key_grad: bfloat16 [4, 8, 512, 2048], P('dp', 'seq')
- value_grad: bfloat16 [4, 8, 512, 2048], P('dp', 'seq')
- wo_grad: float32 [2048, 2048], P(('dp', 'seq'))
Inputs may be any that keep to these rules, and one draw needn't show every extreme that they name: row_mask[a, b] is 1 for b = a and 0 for b > a. col_mask[r, s] is 1 for s = r and for s = r - 1, and 0 for s > r.
All inputs are finite; a program needn't handle non-finite values.
Results may differ from a plain program's by a relative error of at most 0.012.
Values may be sent and summed in bfloat16 or wider, within the bound.
No kernel may reach another device: no remote copies, remote signals or barrier semaphores. Data moves between devices by JAX's collectives and lax.ppermute only.
A program may use at most 192 MiB of HBM per device.

v0:
```python
import math
import jax
import jax.numpy as jnp
from jax import lax
from jax.sharding import PartitionSpec as P

DH = 128
COLS = 512
BLK = 128
masked_out = -1e30
scale = 1.0 / math.sqrt(DH)


def row_permit(row_mask):
    spread = jnp.repeat(jnp.repeat(row_mask, BLK, axis=0), BLK, axis=1)
    row_index = lax.broadcasted_iota(jnp.int32, (COLS, COLS), 0)
    col_index = lax.broadcasted_iota(jnp.int32, (COLS, COLS), 1)
    return (spread == 1) & (col_index <= row_index)


def softmax_parts(scores, allowed):
    highest = jnp.max(jnp.where(allowed, scores, masked_out), axis=-1, keepdims=True)
    attend = jnp.exp(jnp.where(allowed, scores - highest, masked_out))
    totals = jnp.sum(attend, axis=-1, keepdims=True)
    probs = (attend / totals).astype(jnp.bfloat16)
    return (probs, highest + jnp.log(totals))


def row_forward(q, k, v, allowed):
    scores = jnp.einsum("ihd,jhd->hij", q, k, preferred_element_type=jnp.float32) * scale
    probs, log_total = softmax_parts(scores, allowed[None])
    out = jnp.einsum("hij,jhd->ihd", probs, v, preferred_element_type=jnp.float32)
    return (out.astype(jnp.bfloat16), scores, log_total)


def row_backward(q, k, v, out, grad, scores, log_total, allowed):
    grad_dot = jnp.einsum("ihd,ihd->hi", grad, out, preferred_element_type=jnp.float32)
    back = jnp.where(allowed[None], jnp.exp(scores - log_total), 0.0)
    value_grad = jnp.einsum(
        "hij,ihd->jhd", back.astype(jnp.bfloat16), grad, preferred_element_type=jnp.float32
    )
    prob_grad = jnp.einsum("ihd,jhd->hij", grad, v, preferred_element_type=jnp.float32)
    score_grad = (back * (prob_grad - grad_dot[..., None])).astype(jnp.bfloat16)
    query_grad = jnp.einsum("hij,jhd->ihd", score_grad, k, preferred_element_type=jnp.float32)
    key_grad = jnp.einsum("hij,ihd->jhd", score_grad, q, preferred_element_type=jnp.float32)
    return tuple(
        (g.astype(jnp.bfloat16) for g in (query_grad * scale, key_grad * scale, value_grad))
    )


def column_forward(q, k, v, allowed):
    scores = jnp.einsum("rchd,schd->chrs", q, k, preferred_element_type=jnp.float32) * scale
    probs, log_total = softmax_parts(scores, allowed)
    out = jnp.einsum("chrs,schd->rchd", probs, v, preferred_element_type=jnp.float32)
    return (out.astype(jnp.bfloat16), scores, log_total)


def column_backward(q, k, v, out, grad, scores, log_total, allowed):
    grad_dot = jnp.einsum("rchd,rchd->chr", grad, out, preferred_element_type=jnp.float32)
    back = jnp.where(allowed, jnp.exp(scores - log_total), 0.0)
    value_grad = jnp.einsum(
        "chrs,rchd->schd", back.astype(jnp.bfloat16), grad, preferred_element_type=jnp.float32
    )
    prob_grad = jnp.einsum("rchd,schd->chrs", grad, v, preferred_element_type=jnp.float32)
    score_grad = (back * (prob_grad - grad_dot[..., None])).astype(jnp.bfloat16)
    query_grad = jnp.einsum("chrs,schd->rchd", score_grad, k, preferred_element_type=jnp.float32)
    key_grad = jnp.einsum("chrs,rchd->schd", score_grad, q, preferred_element_type=jnp.float32)
    return tuple(
        (g.astype(jnp.bfloat16) for g in (query_grad * scale, key_grad * scale, value_grad))
    )


def on_device(queries, keys, values, out_grad, out_weight, row_mask, col_mask):
    tokens, features = (queries.shape[2], queries.shape[3])
    half = features // 2
    heads_half = half // DH
    rows = lax.axis_size("seq")
    cols_each = tokens // rows
    weight = lax.all_gather(out_weight, "dp", axis=0, tiled=True)
    chunks = 2
    piece = cols_each // chunks

    def chunked(t):
        return t.reshape(rows, chunks, piece, half).transpose(1, 0, 2, 3)

    packed = jnp.stack([chunked(t[0, 0, :, half:]) for t in (queries, keys, values)], axis=1)
    col_ok = col_mask == 1
    shipped_all = [
        lax.all_to_all(packed[j], "seq", split_axis=1, concat_axis=1, tiled=True)
        for j in range(chunks)
    ]
    row_ok = row_permit(row_mask)
    split = lambda t: t[0, 0, :, :half].reshape(tokens, heads_half, DH)
    row_q, row_k, row_v = (split(queries), split(keys), split(values))
    row_out, row_scores, row_total = row_forward(row_q, row_k, row_v, row_ok)
    row_attn = row_out.reshape(tokens, half)
    flat_grad = out_grad[0, 0]
    contract = (((0,), (0,)), ((), ()))
    row_done, shipped_first = lax.optimization_barrier(
        ((row_out, row_scores, row_total), shipped_all[0])
    )
    row_out, row_scores, row_total = row_done
    row_attn = row_out.reshape(tokens, half)
    shipped_all[0] = shipped_first
    col_state = []
    col_back = []
    for j in range(chunks):
        shipped = shipped_all[j]
        col_q, col_k, col_v = (shipped[i].reshape(rows, piece, heads_half, DH) for i in range(3))
        col_out, col_scores, col_total = column_forward(col_q, col_k, col_v, col_ok)
        col_state.append((col_q, col_k, col_v, col_out, col_scores, col_total))
        col_back.append(col_out.reshape(rows, piece, half))
    col_attn = lax.all_to_all(
        jnp.stack(col_back, axis=1), "seq", split_axis=0, concat_axis=0, tiled=True
    ).reshape(tokens, half)
    attention = jnp.concatenate([row_attn, col_attn], axis=1)
    partial = lax.dot_general(attention, flat_grad, contract, preferred_element_type=jnp.float32)
    by_rows_of = (((1,), (1,)), ((), ()))
    row_grad = lax.dot_general(
        flat_grad, weight[:half], by_rows_of, preferred_element_type=jnp.float32
    ).astype(jnp.bfloat16)
    partial, late_weight = lax.optimization_barrier((partial, weight))
    col_grad = lax.dot_general(
        flat_grad, late_weight[half:], by_rows_of, preferred_element_type=jnp.float32
    ).astype(jnp.bfloat16)
    grad_col_part = chunked(col_grad)
    devices_all = lax.axis_size(("dp", "seq"))
    wo_grad = lax.psum_scatter(
        partial.astype(jnp.bfloat16), ("dp", "seq"), scatter_dimension=0, tiled=True
    ).astype(jnp.float32) * (1.0 / math.sqrt(tokens * devices_all))
    col_grads_back = []
    for j in range(chunks):
        grad_cols = lax.all_to_all(
            grad_col_part[j], "seq", split_axis=0, concat_axis=0, tiled=True
        ).reshape(rows, piece, heads_half, DH)
        col_q, col_k, col_v, col_out, col_scores, col_total = col_state[j]
        col_grads = column_backward(
            col_q, col_k, col_v, col_out, grad_cols, col_scores, col_total, col_ok
        )
        col_grads_back.append(
            lax.all_to_all(
                jnp.stack([g.reshape(rows, piece, half) for g in col_grads]),
                "seq",
                split_axis=1,
                concat_axis=1,
                tiled=True,
            )
        )
    col_grads_whole = jnp.stack(col_grads_back, axis=2).reshape(3, tokens, half)
    row_grads = row_backward(
        row_q,
        row_k,
        row_v,
        row_out,
        row_grad.reshape(tokens, heads_half, DH),
        row_scores,
        row_total,
        row_ok,
    )
    layer_out = jnp.dot(attention, weight, preferred_element_type=jnp.float32).astype(jnp.bfloat16)
    grads = [
        jnp.concatenate([row_grads[i].reshape(tokens, half), col_grads_whole[i]], axis=1)[
            None, None
        ]
        for i in range(3)
    ]
    return (layer_out[None, None], grads[0], grads[1], grads[2], wo_grad)


def solution(mesh):
    in_specs = (
        P("dp", "seq", None, None),
        P("dp", "seq", None, None),
        P("dp", "seq", None, None),
        P("dp", "seq", None, None),
        P("dp", None),
        P(),
        P(),
    )
    out_specs = (
        P("dp", "seq", None, None),
        P("dp", "seq", None, None),
        P("dp", "seq", None, None),
        P("dp", "seq", None, None),
        P(("dp", "seq"), None),
    )
    return jax.shard_map(
        on_device, mesh=mesh, in_specs=in_specs, out_specs=out_specs, check_vma=False
    )
```

profile of v0, /device:TPU:0, one launch (start us, length us, event | category | flops | bytes accessed | tf_op | source)
XLA Modules:
  0.0 367.7 jit_solution(15175648478473161992)
XLA Ops:
  7.9 1.9 fusion.99
  15.7 6.3 %all-to-all-start.1 = ((bf16[3,8,32,1024]{3,2,0,1:T(8,128)(2,1)}), bf16[3,8,32,1024]{3,2,0,1:T(8,128)(2,1)}, u32[]{:S(2)}, u32[]{:S(2)}) async-start(bf16[3,8,32,1024]{3,2,0,1:T(8,128)(2,1)} %copy.219), calls=%async_computation.1 | async-start | bytes 3145728 | tf_op jit(solution)/shard_map/all_to_all | solution.py:89
  23.7 1.6 copy.296
  25.3 2.7 copy.297
  28.0 2.7 copy.211
  30.7 29.2 %all-to-all-done.1 = bf16[3,8,32,1024]{3,2,0,1:T(8,128)(2,1)} async-done(((bf16[3,8,32,1024]{3,2,0,1:T(8,128)(2,1)}), bf16[3,8,32,1024]{3,2,0,1:T(8,128)(2,1)}, u32[]{:S(2)}, u32[]{:S(2)}) %all-to-all-start.1) | async-done | bytes 1572896 | tf_op jit(solution)/shard_map/all_to_all | solution.py:89
  59.9 4.6 %all-to-all-start = ((bf16[3,8,32,1024]{3,2,0,1:T(8,128)(2,1)}), bf16[3,8,32,1024]{3,2,0,1:T(8,128)(2,1)}, u32[]{:S(2)}, u32[]{:S(2)}) async-start(bf16[3,8,32,1024]{3,2,0,1:T(8,128)(2,1)} %copy.211), calls=%async_computation | async-start | bytes 3145728 | tf_op jit(solution)/shard_map/all_to_all | solution.py:89
  64.5 2.9 select_reduce_fusion
  70.7 3.6 fusion.36
  78.5 23.8 %all-to-all-done = bf16[3,8,32,1024]{3,2,0,1:T(8,128)(2,1)} async-done(((bf16[3,8,32,1024]{3,2,0,1:T(8,128)(2,1)}), bf16[3,8,32,1024]{3,2,0,1:T(8,128)(2,1)}, u32[]{:S(2)}, u32[]{:S(2)}) %all-to-all-start) | async-done | bytes 1572896 | tf_op jit(solution)/shard_map/all_to_all | solution.py:89
  106.0 2.0 fusion.54
  110.9 2.1 stack_reshape.25
  113.0 2.1 convolution_convert_fusion.4
  116.7 2.0 stack_reshape.24
  121.2 4.2 %all-to-all-start.2 = ((bf16[8,2,32,1024]{3,2,1,0:T(8,128)(2,1)}), bf16[8,2,32,1024]{3,2,1,0:T(8,128)(2,1)}, u32[]{:S(2)}, u32[]{:S(2)}) async-start(bf16[8,2,32,1024]{3,2,1,0:T(8,128)(2,1)} %copy.225), calls=%async_computation.2 | async-start | bytes 2097152 | tf_op jit(solution)/shard_map/all_to_all | solution.py:113
  126.0 2.3 copy.212
  128.3 23.7 %all-to-all-done.2 = bf16[8,2,32,1024]{3,2,1,0:T(8,128)(2,1)} async-done(((bf16[8,2,32,1024]{3,2,1,0:T(8,128)(2,1)}), bf16[8,2,32,1024]{3,2,1,0:T(8,128)(2,1)}, u32[]{:S(2)}, u32[]{:S(2)}) %all-to-all-start.2) | async-done | bytes 1048608 | tf_op jit(solution)/shard_map/all_to_all | solution.py:113
  152.0 2.3 copy.226
  154.3 8.3 %fusion.14 = bf16[2048,2048]{1,0:T(8,128)(2,1)} fusion(bf16[1,1,512,2048]{3,2,1,0:T(8,128)(2,1)S(1)} %copy-done, bf16[512,1024]{0,1:T(8,128)(2,1)} %copy.226, bf16[512,1024]{0,1:T(8,128)(2,1)} %bitcast.241), kind=kOutput, calls=%fused_computation.29 | convolution fusion | flops 4299161600 | bytes 12582912 | tf_op jit(solution)/shard_map/dot_general | solution.py:117
  162.6 4.5 %fusion.18 = bf16[1024,512]{0,1:T(8,128)(2,1)S(1)} fusion(bf16[1,1,512,2048]{3,2,1,0:T(8,128)(2,1)S(1)} %copy-done, bf16[2048,2048]{1,0:T(8,128)(2,1)} %all-gather.2.cloned.1.call-done), kind=kOutput, calls=%fused_computation.42 | convolution fusion | flops 2148007936 | bytes 7340032 | tf_op jit(solution)/shard_map/dot_general | solution.py:123
  168.4 4.2 %all-to-all-start.3 = ((bf16[8,32,1024]{2,1,0:T(8,128)(2,1)}), bf16[8,32,1024]{2,1,0:T(8,128)(2,1)}, u32[]{:S(2)}, u32[]{:S(2)}) async-start(bf16[8,32,1024]{2,1,0:T(8,128)(2,1)} %get-tuple-element.37), calls=%async_computation.3 | async-start | bytes 1048576 | tf_op jit(solution)/shard_map/all_to_all | solution.py:133
  172.5 1.8 log_add_fusion
  174.3 20.8 %all-to-all-done.3 = bf16[8,32,1024]{2,1,0:T(8,128)(2,1)} async-done(((bf16[8,32,1024]{2,1,0:T(8,128)(2,1)}), bf16[8,32,1024]{2,1,0:T(8,128)(2,1)}, u32[]{:S(2)}, u32[]{:S(2)}) %all-to-all-start.3) | async-done | bytes 524320 | tf_op jit(solution)/shard_map/all_to_all | solution.py:133
  195.1 4.2 %all-to-all-start.5 = ((bf16[8,32,1024]{2,1,0:T(8,128)(2,1)}), bf16[8,32,1024]{2,1,0:T(8,128)(2,1)}, u32[]{:S(2)}, u32[]{:S(2)}) async-start(bf16[8,32,1024]{2,1,0:T(8,128)(2,1)} %get-tuple-element.36), calls=%async_computation.5 | async-start | bytes 1048576 | tf_op jit(solution)/shard_map/all_to_all | solution.py:133
  201.2 1.9 fusion.49
  203.9 2.1 stack_reshape.28
  207.3 1.7 multiply_reduce_fusion.2
  212.1 2.1 stack_reshape.26
  214.2 1.7 fusion.47
  216.8 2.1 stack_reshape.27
  223.0 4.5 %all-to-all-start.4 = ((bf16[3,8,32,1024]{3,2,0,1:T(8,128)(2,1)}), bf16[3,8,32,1024]{3,2,0,1:T(8,128)(2,1)}, u32[]{:S(2)}, u32[]{:S(2)}) async-start(bf16[3,8,32,1024]{3,2,0,1:T(8,128)(2,1)} %copy.242), calls=%async_computation.4 | async-start | bytes 3145728 | tf_op jit(solution)/shard_map/all_to_all | solution.py:141
  227.5 4.6 %fusion.31 = bf16[64,8,8,128]{3,1,2,0:T(8,128)(2,1)S(1)} fusion(bf16[2048,2048]{1,0:T(8,128)(2,1)} %all-gather.2.cloned.1.call-done, bf16[1,1,512,2048]{3,2,1,0:T(8,128)(2,1)S(1)} %copy-done), kind=kOutput, calls=%fused_computation.45 | convolution fusion | flops 2148007936 | bytes 7340032 | tf_op jit(solution)/shard_map/dot_general | solution.py:119
  233.4 2.4 copy.259
  241.6 2.1 stack_reshape.31
  244.9 1.7 multiply_reduce_fusion.1
  249.8 2.1 stack_reshape.29
  256.5 26.0 %all-to-all-done.4 = bf16[3,8,32,1024]{3,2,0,1:T(8,128)(2,1)} async-done(((bf16[3,8,32,1024]{3,2,0,1:T(8,128)(2,1)}), bf16[3,8,32,1024]{3,2,0,1:T(8,128)(2,1)}, u32[]{:S(2)}, u32[]{:S(2)}) %all-to-all-start.4) | async-done | bytes 1572896 | tf_op jit(solution)/shard_map/all_to_all | solution.py:141
  282.4 5.8 %all-to-all-start.6 = ((bf16[3,8,32,1024]{3,2,0,1:T(8,128)(2,1)}), bf16[3,8,32,1024]{3,2,0,1:T(8,128)(2,1)}, u32[]{:S(2)}, u32[]{:S(2)}) async-start(bf16[3,8,32,1024]{3,2,0,1:T(8,128)(2,1)} %copy.254), calls=%async_computation.6 | async-start | bytes 3145728 | tf_op jit(solution)/shard_map/all_to_all | solution.py:141
  288.3 5.5 %multiply_convert_fusion = bf16[8,512,512]{1,2,0:T(8,128)(2,1)S(1)} fusion(f32[8,512,512]{1,2,0:T(8,128)} %copy-done.1, f32[8,512]{1,0:T(8,128)S(1)} %multiply_reduce_fusion, f32[8,512]{1,0:T(8,128)S(1)} %bitcast.246, pred[512,512]{0,1:T(8,128)(4,1)S(1)} %fusion.53, bf16[512,8,128]{0,2,1:T(8,128)(2,1)} %copy.259, bf16[512,8,128]{0,2,1:T(8,128)(2,1)S(1)} %bitcast.214), kind=kOutput, calls=%fused_computation | convolution fusion | flops 547356672 | bytes 14974976 | tf_op jit(solution)/shard_map/ihd,jhd->hij/dot_general | solution.py:42
  297.2 5.1 %multiply_convert_fusion.1 = bf16[8,512,128]{1,2,0:T(8,128)(2,1)} fusion(bf16[8,512,512]{1,2,0:T(8,128)(2,1)} %copy-done.2, bf16[512,8,128]{0,2,1:T(8,128)(2,1)} %bitcast.224), kind=kOutput, calls=%fused_computation.33 | convolution fusion | flops 537919488 | bytes 6291456 | tf_op jit(solution)/shard_map/hij,ihd->jhd/dot_general | solution.py:45
  302.3 2.3 copy.258
  304.6 6.0 %fusion.28 = bf16[8,128,512]{2,1,0:T(8,128)(2,1)} fusion(bf16[512,8,128]{0,2,1:T(8,128)(2,1)S(1)} %copy-done.20, f32[8,512,512]{1,2,0:T(8,128)} %copy-done.1, f32[8,512]{1,0:T(8,128)S(1)} %bitcast.247, pred[512,512]{0,1:T(8,128)(4,1)S(1)} %fusion.53), kind=kOutput, calls=%fused_computation.44 | convolution fusion | flops 543686656 | bytes 10764288 | tf_op jit(solution)/shard_map/hij,ihd->jhd/dot_general | solution.py:39
  312.1 10.0 %fusion.12 = bf16[1,1,512,2048]{3,2,1,0:T(8,128)(2,1)} fusion(bf16[2048,2048]{1,0:T(8,128)(2,1)} %all-gather.2.cloned.1.call-done, bf16[512,1024]{0,1:T(8,128)(2,1)} %copy.226, bf16[512,1024]{0,1:T(8,128)(2,1)} %bitcast.242), kind=kOutput, calls=%fused_computation.23 | convolution fusion | flops 4300210176 | bytes 12582912 | tf_op jit(solution)/shard_map/dot_general | solution.py:160
  322.0 2.8 copy.356
  324.8 19.7 %all-to-all-done.6 = bf16[3,8,32,1024]{3,2,0,1:T(8,128)(2,1)} async-done(((bf16[3,8,32,1024]{3,2,0,1:T(8,128)(2,1)}), bf16[3,8,32,1024]{3,2,0,1:T(8,128)(2,1)}, u32[]{:S(2)}, u32[]{:S(2)}) %all-to-all-start.6) | async-done | bytes 1572896 | tf_op jit(solution)/shard_map/all_to_all | solution.py:141
  344.5 1.7 copy.355
  351.2 7.6 %reduce-scatter.2.cloned.1.call-done = bf16[64,2048]{1,0:T(8,128)(2,1)} async-done(((bf16[2048,2048]{1,0:T(8,128)(2,1)}), bf16[64,2048]{1,0:T(8,128)(2,1)}) %reduce-scatter.2.cloned.1.call-update) | async-done | bytes 262160 | tf_op jit(solution)/shard_map/reduce_scatter | solution.py:128
  358.8 1.8 convert_multiply_fusion
  (157 shorter events, 65.9 us)
Async XLA Ops:
  7.2 147.1 %copy-start = (bf16[1,1,512,2048]{3,2,1,0:T(8,128)(2,1)S(1)}, bf16[1,1,512,2048]{3,2,1,0:T(8,128)(2,1)}, u32[]{:S(2)}) copy-start(bf16[1,1,512,2048]{3,2,1,0:T(8,128)(2,1)} %param.10) | copy-start | bytes 6291460
  7.2 155.4 %all-gather.2.cloned.1.call-start = ((), (), s32[]{:S(2)}) async-start(), calls=%async_computation.8 | async-start | bytes 10485760 | tf_op jit(solution)/shard_map/all_gather | solution.py:79
  7.9 2.2 copy-start.27
  7.9 3.4 copy-start.28
  14.3 7.6 %copy-start.43 = (s32[4,4]{1,0:T(4,128)S(1)}, s32[4,4]{1,0:T(4,128)}, u32[]{:S(2)}) copy-start(s32[4,4]{1,0:T(4,128)} %param.12) | copy-start | bytes 196
  14.4 7.8 %copy-start.42 = (s32[8,8]{1,0:T(8,128)S(1)}, s32[8,8]{1,0:T(8,128)}, u32[]{:S(2)}) copy-start(s32[8,8]{1,0:T(8,128)} %param.13) | copy-start | bytes 772
  15.7 44.3 %all-to-all-start.1 = ((bf16[3,8,32,1024]{3,2,0,1:T(8,128)(2,1)}), bf16[3,8,32,1024]{3,2,0,1:T(8,128)(2,1)}, u32[]{:S(2)}, u32[]{:S(2)}) async-start(bf16[3,8,32,1024]{3,2,0,1:T(8,128)(2,1)} %copy.219), calls=%async_computation.1 | async-start | bytes 3145728 | tf_op jit(solution)/shard_map/all_to_all | solution.py:89
  22.2 186.8 %copy-start.39 = (pred[8,8]{0,1:T(8,128)(4,1)}, pred[8,8]{0,1:T(8,128)(4,1)S(1)}, u32[]{:S(2)}) copy-start(pred[8,8]{0,1:T(8,128)(4,1)S(1)} %copy.213) | copy-start | bytes 196
  25.3 39.2 %copy-start.5 = (bf16[1,1,512,1024]{2,3,1,0:T(8,128)(2,1)}, bf16[1,1,512,1024]{2,3,1,0:T(8,128)(2,1)S(1)}, u32[]{:S(2)}) copy-start(bf16[1,1,512,1024]{2,3,1,0:T(8,128)(2,1)S(1)} %copy.296) | copy-start | bytes 3145732
  59.9 42.4 %all-to-all-start = ((bf16[3,8,32,1024]{3,2,0,1:T(8,128)(2,1)}), bf16[3,8,32,1024]{3,2,0,1:T(8,128)(2,1)}, u32[]{:S(2)}, u32[]{:S(2)}) async-start(bf16[3,8,32,1024]{3,2,0,1:T(8,128)(2,1)} %copy.211), calls=%async_computation | async-start | bytes 3145728 | tf_op jit(solution)/shard_map/all_to_all | solution.py:89
  67.4 3.3 copy-start.1
  67.4 3.3 copy-start.18
  103.9 2.1 copy-start.14
  103.9 2.1 copy-start.16
  104.9 1.1 copy-start.25
  105.0 1.0 copy-start.24
  105.0 3.5 copy-start.31
  105.9 3.3 copy-start.3
  105.9 7.0 %copy-start.37 = (f32[32,8,8]{2,1,0:T(8,128)}, f32[32,8,8]{2,1,0:T(8,128)S(1)}, u32[]{:S(2)}) copy-start(f32[32,8,8]{2,1,0:T(8,128)S(1)} %get-tuple-element.40) | copy-start | bytes 24580
  108.0 1.2 copy-start.34
  109.2 0.8 copy-start.29
  115.0 0.8 copy-start.30
  121.2 30.8 %all-to-all-start.2 = ((bf16[8,2,32,1024]{3,2,1,0:T(8,128)(2,1)}), bf16[8,2,32,1024]{3,2,1,0:T(8,128)(2,1)}, u32[]{:S(2)}, u32[]{:S(2)}) async-start(bf16[8,2,32,1024]{3,2,1,0:T(8,128)(2,1)} %copy.225), calls=%async_computation.2 | async-start | bytes 2097152 | tf_op jit(solution)/shard_map/all_to_all | solution.py:113
  125.4 233.4 %reduce-scatter.2.cloned.1.call-start = ((), (), s32[]{:S(2)}) async-start(), calls=%async_computation.9 | async-start | bytes 8650752 | tf_op jit(solution)/shard_map/reduce_scatter | solution.py:128
  168.4 26.7 %all-to-all-start.3 = ((bf16[8,32,1024]{2,1,0:T(8,128)(2,1)}), bf16[8,32,1024]{2,1,0:T(8,128)(2,1)}, u32[]{:S(2)}, u32[]{:S(2)}) async-start(bf16[8,32,1024]{2,1,0:T(8,128)(2,1)} %get-tuple-element.37), calls=%async_computation.3 | async-start | bytes 1048576 | tf_op jit(solution)/shard_map/all_to_all | solution.py:133
  195.1 27.9 %all-to-all-start.5 = ((bf16[8,32,1024]{2,1,0:T(8,128)(2,1)}), bf16[8,32,1024]{2,1,0:T(8,128)(2,1)}, u32[]{:S(2)}, u32[]{:S(2)}) async-start(bf16[8,32,1024]{2,1,0:T(8,128)(2,1)} %get-tuple-element.36), calls=%async_computation.5 | async-start | bytes 1048576 | tf_op jit(solution)/shard_map/all_to_all | solution.py:133
  206.0 3.0 copy-start.4
  206.0 3.1 copy-start.10
  206.0 3.1 copy-start.33
  206.0 3.1 copy-start.35
  206.0 4.7 %copy-start.26 = (bf16[32,8,8,128]{3,2,1,0:T(8,128)(2,1)S(1)}, bf16[32,8,8,128]{3,2,1,0:T(8,128)(2,1)}, u32[]{:S(2)}) copy-start(bf16[32,8,8,128]{3,2,1,0:T(8,128)(2,1)} %copy-done.25) | copy-start | bytes 1572868
  223.0 59.4 %all-to-all-start.4 = ((bf16[3,8,32,1024]{3,2,0,1:T(8,128)(2,1)}), bf16[3,8,32,1024]{3,2,0,1:T(8,128)(2,1)}, u32[]{:S(2)}, u32[]{:S(2)}) async-start(bf16[3,8,32,1024]{3,2,0,1:T(8,128)(2,1)} %copy.242), calls=%async_computation.4 | async-start | bytes 3145728 | tf_op jit(solution)/shard_map/all_to_all | solution.py:141
  235.8 1.5 copy-start.21
  235.8 4.3 %copy-start.40 = (pred[8,8]{0,1:T(8,128)(4,1)S(1)}, pred[8,8]{0,1:T(8,128)(4,1)}, u32[]{:S(2)}) copy-start(pred[8,8]{0,1:T(8,128)(4,1)} %copy-done.39) | copy-start | bytes 196
  243.7 3.0 copy-start.8
  243.7 3.0 copy-start.32
  243.7 3.0 copy-start.41
  243.7 4.7 %copy-start.17 = (bf16[32,8,8,128]{3,2,1,0:T(8,128)(2,1)S(1)}, bf16[32,8,8,128]{3,2,1,0:T(8,128)(2,1)}, u32[]{:S(2)}) copy-start(bf16[32,8,8,128]{3,2,1,0:T(8,128)(2,1)} %copy.304) | copy-start | bytes 1572868
  248.4 3.5 copy-start.15
  255.1 33.1 %copy-start.19 = (bf16[1,1,512,1024]{2,3,1,0:T(8,128)(2,1)S(1)}, bf16[1,1,512,1024]{2,3,1,0:T(8,128)(2,1)}, u32[]{:S(2)}) copy-start(bf16[1,1,512,1024]{2,3,1,0:T(8,128)(2,1)} %copy.297) | copy-start | bytes 3145732
  255.1 33.1 %copy-start.38 = (f32[8,512,1]{1,0,2:T(8,128)S(1)}, f32[8,512,1]{1,0,2:T(8,128)}, u32[]{:S(2)}) copy-start(f32[8,512,1]{1,0,2:T(8,128)} %add_bitcast_fusion) | copy-start | bytes 49156
  282.4 62.1 %all-to-all-start.6 = ((bf16[3,8,32,1024]{3,2,0,1:T(8,128)(2,1)}), bf16[3,8,32,1024]{3,2,0,1:T(8,128)(2,1)}, u32[]{:S(2)}, u32[]{:S(2)}) async-start(bf16[3,8,32,1024]{3,2,0,1:T(8,128)(2,1)} %copy.254), calls=%async_computation.6 | async-start | bytes 3145728 | tf_op jit(solution)/shard_map/all_to_all | solution.py:141
  288.3 5.6 %copy-start.6 = (bf16[1,1,512,1024]{2,3,1,0:T(8,128)(2,1)S(1)}, bf16[1,1,512,1024]{2,3,1,0:T(8,128)(2,1)}, u32[]{:S(2)}) copy-start(bf16[1,1,512,1024]{2,3,1,0:T(8,128)(2,1)} %copy-done.5) | copy-start | bytes 3145732
  293.8 2.0 copy-start.2
  297.2 7.3 %copy-start.20 = (bf16[512,8,128]{0,2,1:T(8,128)(2,1)S(1)}, bf16[512,8,128]{0,2,1:T(8,128)(2,1)}, u32[]{:S(2)}) copy-start(bf16[512,8,128]{0,2,1:T(8,128)(2,1)} %copy.259) | copy-start | bytes 3145732
  344.5 1.9 copy-start.11
  346.7 1.5 copy-start.22
  348.2 1.5 copy-start.23
  (5 other events, 3.9 us)
Sparse Core Ops, SparseCore 0:
  9.9 90.2 all-gather.1
  162.8 196.0 reduce-scatter.1
where the time goes:
time: 372 us; the launch traced here: 368 us
  waiting for transfers between devices  153 us (41%)
  local copies, waits for them, and re-layouts  75.6 us (20%)
  matrix products  65.5 us (18%)
  starting transfers between devices  34.4 us (9%)
  other arithmetic  24.4 us (7%)
  between operations  15 us (4%)
    all_to_all x2, waiting for transfers between devices, on_device(): lax.all_to_all(packed[j], 'seq', split_axis=1, concat_axis=1, tiled=True)  53 us
    all_to_all x2, waiting for transfers between devices, on_device(): lax.all_to_all(jnp.stack([g.reshape(rows, piece, half) for g in col_grads...  45.6 us
    all_to_all x1, waiting for transfers between devices, on_device(): lax.all_to_all(jnp.stack(col_back, axis=1), 'seq', split_axis=0, concat_a...  23.7 us
    all_to_all x2, waiting for transfers between devices, on_device(): lax.all_to_all(grad_col_part[j], 'seq', split_axis=0, concat_axis=0, tile...  22.1 us
    unnamed x102, local copies, waits for them, and re-layouts  20.3 us
    another operation x8, local copies, waits for them, and re-layouts, on_device(): jnp.stack([g.reshape(rows, piece, half) for g in col_grads])  13.2 us
    all_to_all x2, starting transfers between devices, on_device(): lax.all_to_all(packed[j], 'seq', split_axis=1, concat_axis=1, tiled=True)  10.9 us
    all_to_all x2, starting transfers between devices, on_device(): lax.all_to_all(jnp.stack([g.reshape(rows, piece, half) for g in col_grads...  10.3 us
  transfers between devices with their start and end apart: 9, of which 8 were waited for; matrix products, arithmetic and copies ran while one was open for 43% of the time, Pallas kernels for 0%

commit v1 on v0

--- a/solution.py
+++ b/solution.py
@@ -9,6 +9,12 @@
 BLK = 128
 masked_out = -1e30
 scale = 1.0 / math.sqrt(DH)
+
+
+def stacked_exchange(x, axis, split, join):
+    cells = jnp.split(x, lax.axis_size(axis), axis=split)
+    received = lax.all_to_all(jnp.stack(cells), axis, 0, 0)
+    return jnp.concatenate(received, axis=join)
 
 
 def row_permit(row_mask):
@@ -138,12 +144,8 @@
             col_q, col_k, col_v, col_out, grad_cols, col_scores, col_total, col_ok
         )
         col_grads_back.append(
-            lax.all_to_all(
-                jnp.stack([g.reshape(rows, piece, half) for g in col_grads]),
-                "seq",
-                split_axis=1,
-                concat_axis=1,
-                tiled=True,
+            stacked_exchange(
+                jnp.stack([g.reshape(rows, piece, half) for g in col_grads]), "seq", 1, 1
             )
         )
     col_grads_whole = jnp.stack(col_grads_back, axis=2).reshape(3, tokens, half)

time: 372 us -> 383 us (1.030)
  waiting for transfers between devices: 153 us -> 175 us
  other arithmetic: 24.4 us -> 20 us
    all_to_all x2, waiting for transfers between devices: 45.6 us -> 62.3 us  [stacked_exchange(): received = lax.all_to_all(jnp.stack(cells), axis, 0, 0)]
    all_to_all x2, waiting for transfers between devices: 22.1 us -> 35 us  [on_device(): lax.all_to_all(grad_col_part[j], 'seq', split_axis=0, concat_axis=0, tile...]
    unnamed x102 -> x118, local copies, waits for them, and re-layouts: 20.3 us -> 30.4 us
    reduce_scatter x1, waiting for transfers between devices: 7.6 us -> 0.01 us  [on_device(): lax.psum_scatter(partial.astype(jnp.bfloat16), ('dp', 'seq'), scatter_dim...]
    another operation x8 -> x7, local copies, waits for them, and re-layouts: 13.2 us -> 6.9 us  [on_device(): jnp.stack([g.reshape(rows, piece, half) for g in col_grads])]
    all_to_all x2 -> x0, local copies, waits for them, and re-layouts: 4.42 us -> none  [on_device(): lax.all_to_all(jnp.stack([g.reshape(rows, piece, half) for g in col_grads...]
  transfers between devices with their start and end apart: 9 -> 9, of which waited for: 8 -> 7; matrix products, arithmetic and copies ran while one was open for 43% -> 38% of each run, Pallas kernels for 0% -> 0%
where the time goes in v1:
time: 383 us; the launch traced here: 379 us
  waiting for transfers between devices  175 us (46%)
  local copies, waits for them, and re-layouts  72 us (19%)
  matrix products  61.7 us (16%)
  starting transfers between devices  34.9 us (9%)
  other arithmetic  20 us (5%)
  between operations  15 us (4%)
    all_to_all x2, waiting for transfers between devices, stacked_exchange(): received = lax.all_to_all(jnp.stack(cells), axis, 0, 0)  62.3 us
    all_to_all x2, waiting for transfers between devices, on_device(): lax.all_to_all(packed[j], 'seq', split_axis=1, concat_axis=1, tiled=True)  53.1 us
    all_to_all x2, waiting for transfers between devices, on_device(): lax.all_to_all(grad_col_part[j], 'seq', split_axis=0, concat_axis=0, tile...  35 us
    unnamed x118, local copies, waits for them, and re-layouts  30.4 us
    all_to_all x1, waiting for transfers between devices, on_device(): lax.all_to_all(jnp.stack(col_back, axis=1), 'seq', split_axis=0, concat_a...  24.1 us
    all_to_all x2, starting transfers between devices, on_device(): lax.all_to_all(packed[j], 'seq', split_axis=1, concat_axis=1, tiled=True)  11.2 us
    all_to_all x2, starting transfers between devices, stacked_exchange(): received = lax.all_to_all(jnp.stack(cells), axis, 0, 0)  10.9 us
    dot_general x1, matrix products, on_device(): jnp.dot(attention, weight, preferred_element_type=jnp.float32)  9.63 us
  transfers between devices with their start and end apart: 9, of which 7 were waited for; matrix products, arithmetic and copies ran while one was open for 38% of the time, Pallas kernels for 0%

profile of v1, /device:TPU:0, one launch (start us, length us, event | category | flops | bytes accessed | tf_op | source)
XLA Modules:
  0.0 378.8 jit_solution(5496500957778373669)
XLA Ops:
  7.9 1.9 fusion.115
  13.6 1.6 slice_bitcast_fusion.1
  16.5 6.5 %all-to-all-start.1 = ((bf16[3,8,32,1024]{3,2,0,1:T(8,128)(2,1)}), bf16[3,8,32,1024]{3,2,0,1:T(8,128)(2,1)}, u32[]{:S(2)}, u32[]{:S(2)}) async-start(bf16[3,8,32,1024]{3,2,0,1:T(8,128)(2,1)} %copy.256), calls=%async_computation.1 | async-start | bytes 3145728 | tf_op jit(solution)/shard_map/all_to_all | solution.py:95
  24.7 1.5 copy.339
  26.2 2.7 copy.340
  28.8 2.7 copy.248
  31.6 29.3 %all-to-all-done.1 = bf16[3,8,32,1024]{3,2,0,1:T(8,128)(2,1)} async-done(((bf16[3,8,32,1024]{3,2,0,1:T(8,128)(2,1)}), bf16[3,8,32,1024]{3,2,0,1:T(8,128)(2,1)}, u32[]{:S(2)}, u32[]{:S(2)}) %all-to-all-start.1) | async-done | bytes 1572896 | tf_op jit(solution)/shard_map/all_to_all | solution.py:95
  60.9 4.8 %all-to-all-start = ((bf16[3,8,32,1024]{3,2,0,1:T(8,128)(2,1)}), bf16[3,8,32,1024]{3,2,0,1:T(8,128)(2,1)}, u32[]{:S(2)}, u32[]{:S(2)}) async-start(bf16[3,8,32,1024]{3,2,0,1:T(8,128)(2,1)} %copy.248), calls=%async_computation | async-start | bytes 3145728 | tf_op jit(solution)/shard_map/all_to_all | solution.py:95
  65.7 2.9 select_reduce_fusion
  71.8 3.6 fusion.36
  75.4 1.5 fusion.118
  79.7 23.8 %all-to-all-done = bf16[3,8,32,1024]{3,2,0,1:T(8,128)(2,1)} async-done(((bf16[3,8,32,1024]{3,2,0,1:T(8,128)(2,1)}), bf16[3,8,32,1024]{3,2,0,1:T(8,128)(2,1)}, u32[]{:S(2)}, u32[]{:S(2)}) %all-to-all-start) | async-done | bytes 1572896 | tf_op jit(solution)/shard_map/all_to_all | solution.py:95
  103.5 1.5 fusion.117
  107.5 2.0 fusion.54
  112.4 2.1 stack_reshape.25
  114.5 2.1 convolution_convert_fusion.4
  118.2 2.1 stack_reshape.24
  122.6 4.2 %all-to-all-start.2 = ((bf16[8,2,32,1024]{3,2,1,0:T(8,128)(2,1)}), bf16[8,2,32,1024]{3,2,1,0:T(8,128)(2,1)}, u32[]{:S(2)}, u32[]{:S(2)}) async-start(bf16[8,2,32,1024]{3,2,1,0:T(8,128)(2,1)} %copy.262), calls=%async_computation.2 | async-start | bytes 2097152 | tf_op jit(solution)/shard_map/all_to_all | solution.py:119
  127.1 2.3 copy.249
  129.4 24.1 %all-to-all-done.2 = bf16[8,2,32,1024]{3,2,1,0:T(8,128)(2,1)} async-done(((bf16[8,2,32,1024]{3,2,1,0:T(8,128)(2,1)}), bf16[8,2,32,1024]{3,2,1,0:T(8,128)(2,1)}, u32[]{:S(2)}, u32[]{:S(2)}) %all-to-all-start.2) | async-done | bytes 1048608 | tf_op jit(solution)/shard_map/all_to_all | solution.py:119
  153.5 2.3 copy.263
  155.8 8.3 %fusion.14 = bf16[2048,2048]{1,0:T(8,128)(2,1)} fusion(bf16[1,1,512,2048]{3,2,1,0:T(8,128)(2,1)S(1)} %copy-done, bf16[512,1024]{0,1:T(8,128)(2,1)} %copy.263, bf16[512,1024]{0,1:T(8,128)(2,1)} %bitcast.319), kind=kOutput, calls=%fused_computation.29 | convolution fusion | flops 4299161600 | bytes 12582912 | tf_op jit(solution)/shard_map/dot_general | solution.py:123
  164.1 4.5 %fusion.18 = bf16[1024,512]{0,1:T(8,128)(2,1)S(1)} fusion(bf16[1,1,512,2048]{3,2,1,0:T(8,128)(2,1)S(1)} %copy-done, bf16[2048,2048]{1,0:T(8,128)(2,1)} %all-gather.2.cloned.1.call-done), kind=kOutput, calls=%fused_computation.39 | convolution fusion | flops 2148007936 | bytes 7340032 | tf_op jit(solution)/shard_map/dot_general | solution.py:129
  169.9 4.2 %all-to-all-start.5 = ((bf16[8,32,1024]{2,1,0:T(8,128)(2,1)}), bf16[8,32,1024]{2,1,0:T(8,128)(2,1)}, u32[]{:S(2)}, u32[]{:S(2)}) async-start(bf16[8,32,1024]{2,1,0:T(8,128)(2,1)} %get-tuple-element.36), calls=%async_computation.5 | async-start | bytes 1048576 | tf_op jit(solution)/shard_map/all_to_all | solution.py:139
  174.0 1.8 log_add_fusion
  175.8 20.8 %all-to-all-done.5 = bf16[8,32,1024]{2,1,0:T(8,128)(2,1)} async-done(((bf16[8,32,1024]{2,1,0:T(8,128)(2,1)}), bf16[8,32,1024]{2,1,0:T(8,128)(2,1)}, u32[]{:S(2)}, u32[]{:S(2)}) %all-to-all-start.5) | async-done | bytes 524320 | tf_op jit(solution)/shard_map/all_to_all | solution.py:139
  196.6 4.1 %all-to-all-start.3 = ((bf16[8,32,1024]{2,1,0:T(8,128)(2,1)}), bf16[8,32,1024]{2,1,0:T(8,128)(2,1)}, u32[]{:S(2)}, u32[]{:S(2)}) async-start(bf16[8,32,1024]{2,1,0:T(8,128)(2,1)} %get-tuple-element.37), calls=%async_computation.3 | async-start | bytes 1048576 | tf_op jit(solution)/shard_map/all_to_all | solution.py:139
  200.8 4.6 %fusion.31 = bf16[64,8,8,128]{3,1,2,0:T(8,128)(2,1)S(1)} fusion(bf16[2048,2048]{1,0:T(8,128)(2,1)} %all-gather.2.cloned.1.call-done, bf16[1,1,512,2048]{3,2,1,0:T(8,128)(2,1)S(1)} %copy-done), kind=kOutput, calls=%fused_computation.42 | convolution fusion | flops 2148007936 | bytes 7340032 | tf_op jit(solution)/shard_map/dot_general | solution.py:125
  210.3 14.3 %all-to-all-done.3 = bf16[8,32,1024]{2,1,0:T(8,128)(2,1)} async-done(((bf16[8,32,1024]{2,1,0:T(8,128)(2,1)}), bf16[8,32,1024]{2,1,0:T(8,128)(2,1)}, u32[]{:S(2)}, u32[]{:S(2)}) %all-to-all-start.3) | async-done | bytes 524320 | tf_op jit(solution)/shard_map/all_to_all | solution.py:139
  227.8 2.1 stack_reshape.28
  229.9 1.5 fusion.50
  232.3 2.1 stack_reshape.31
  234.4 1.8 multiply_reduce_fusion.1
  239.4 2.1 stack_reshape.29
  249.8 4.7 %all-to-all-start.6 = ((bf16[8,3,1,32,1024]{4,3,1,2,0:T(8,128)(2,1)}), bf16[8,3,1,32,1024]{4,3,1,2,0:T(8,128)(2,1)}, u32[]{:S(2)}, u32[]{:S(2)}) async-start(bf16[8,3,1,32,1024]{4,3,1,2,0:T(8,128)(2,1)} %fusion.90), calls=%async_computation.6 | async-start | bytes 3145728 | tf_op jit(solution)/shard_map/all_to_all | solution.py:16
  264.5 46.5 %all-to-all-done.6 = bf16[8,3,1,32,1024]{4,3,1,2,0:T(8,128)(2,1)} async-done(((bf16[8,3,1,32,1024]{4,3,1,2,0:T(8,128)(2,1)}), bf16[8,3,1,32,1024]{4,3,1,2,0:T(8,128)(2,1)}, u32[]{:S(2)}, u32[]{:S(2)}) %all-to-all-start.6) | async-done | bytes 1572896 | tf_op jit(solution)/shard_map/all_to_all | solution.py:16
  311.1 6.2 %all-to-all-start.4 = ((bf16[8,3,1,32,1024]{4,3,1,2,0:T(8,128)(2,1)}), bf16[8,3,1,32,1024]{4,3,1,2,0:T(8,128)(2,1)}, u32[]{:S(2)}, u32[]{:S(2)}) async-start(bf16[8,3,1,32,1024]{4,3,1,2,0:T(8,128)(2,1)} %fusion.98), calls=%async_computation.4 | async-start | bytes 3145728 | tf_op jit(solution)/shard_map/all_to_all | solution.py:16
  317.3 5.1 %multiply_convert_fusion = bf16[8,512,512]{1,2,0:T(8,128)(2,1)S(1)} fusion(f32[8,512,512]{1,2,0:T(8,128)} %copy-done.2, f32[8,512]{1,0:T(8,128)S(1)} %multiply_reduce_fusion, f32[8,512]{1,0:T(8,128)S(1)} %bitcast.324, pred[512,512]{0,1:T(8,128)(4,1)S(1)} %fusion.53, bf16[512,8,128]{0,2,1:T(8,128)(2,1)S(1)} %copy-done.16, bf16[512,8,128]{0,2,1:T(8,128)(2,1)S(1)} %bitcast.289), kind=kOutput, calls=%fused_computation | convolution fusion | flops 547356672 | bytes 14974976 | tf_op jit(solution)/shard_map/ihd,jhd->hij/dot_general | solution.py:48
  325.0 4.0 %multiply_convert_fusion.1 = bf16[8,512,128]{1,2,0:T(8,128)(2,1)S(1)} fusion(bf16[8,512,512]{1,2,0:T(8,128)(2,1)} %copy-done.3, bf16[512,8,128]{0,2,1:T(8,128)(2,1)} %bitcast.299), kind=kOutput, calls=%fused_computation.33 | convolution fusion | flops 537919488 | bytes 6291456 | tf_op jit(solution)/shard_map/hij,ihd->jhd/dot_general | solution.py:51
  330.3 6.0 %fusion.28 = bf16[8,128,512]{2,1,0:T(8,128)(2,1)} fusion(bf16[512,8,128]{0,2,1:T(8,128)(2,1)S(1)} %copy-done.16, f32[8,512,512]{1,2,0:T(8,128)} %copy-done.2, f32[8,512]{1,0:T(8,128)S(1)} %bitcast.325, pred[512,512]{0,1:T(8,128)(4,1)S(1)} %fusion.53), kind=kOutput, calls=%fused_computation.41 | convolution fusion | flops 543686656 | bytes 10764288 | tf_op jit(solution)/shard_map/hij,ihd->jhd/dot_general | solution.py:45
  336.3 1.6 copy.304
  337.9 9.6 %fusion.12 = bf16[1,1,512,2048]{3,2,1,0:T(8,128)(2,1)} fusion(bf16[2048,2048]{1,0:T(8,128)(2,1)} %all-gather.2.cloned.1.call-done, bf16[512,1024]{0,1:T(8,128)(2,1)} %copy.263, bf16[512,1024]{0,1:T(8,128)(2,1)S(1)} %bitcast.320), kind=kOutput, calls=%fused_computation.23 | convolution fusion | flops 4300210176 | bytes 12582912 | tf_op jit(solution)/shard_map/dot_general | solution.py:162
  347.5 15.7 %all-to-all-done.4 = bf16[8,3,1,32,1024]{4,3,1,2,0:T(8,128)(2,1)} async-done(((bf16[8,3,1,32,1024]{4,3,1,2,0:T(8,128)(2,1)}), bf16[8,3,1,32,1024]{4,3,1,2,0:T(8,128)(2,1)}, u32[]{:S(2)}, u32[]{:S(2)}) %all-to-all-start.4) | async-done | bytes 1572896 | tf_op jit(solution)/shard_map/all_to_all | solution.py:16
  363.3 2.1 pad_maximum_fusion.5
  365.4 1.5 maximum_bitcast_fusion.2
  366.9 1.5 maximum_bitcast_fusion
  368.4 1.5 maximum_bitcast_fusion.1
  369.9 1.8 convert_multiply_fusion
  (171 shorter events, 58.6 us)
Async XLA Ops:
  7.2 148.6 %copy-start = (bf16[1,1,512,2048]{3,2,1,0:T(8,128)(2,1)S(1)}, bf16[1,1,512,2048]{3,2,1,0:T(8,128)(2,1)}, u32[]{:S(2)}) copy-start(bf16[1,1,512,2048]{3,2,1,0:T(8,128)(2,1)} %param.10) | copy-start | bytes 6291460
  7.2 156.9 %all-gather.2.cloned.1.call-start = ((), (), s32[]{:S(2)}) async-start(), calls=%async_computation.8 | async-start | bytes 10485760 | tf_op jit(solution)/shard_map/all_gather | solution.py:85
  7.9 2.2 copy-start.23
  10.1 2.0 copy-start.24
  16.5 6.5 %copy-start.43 = (s32[4,4]{1,0:T(4,128)S(1)}, s32[4,4]{1,0:T(4,128)}, u32[]{:S(2)}) copy-start(s32[4,4]{1,0:T(4,128)} %param.12) | copy-start | bytes 196
  16.5 6.6 %copy-start.42 = (s32[8,8]{1,0:T(8,128)S(1)}, s32[8,8]{1,0:T(8,128)}, u32[]{:S(2)}) copy-start(s32[8,8]{1,0:T(8,128)} %param.13) | copy-start | bytes 772
  16.5 44.4 %all-to-all-start.1 = ((bf16[3,8,32,1024]{3,2,0,1:T(8,128)(2,1)}), bf16[3,8,32,1024]{3,2,0,1:T(8,128)(2,1)}, u32[]{:S(2)}, u32[]{:S(2)}) async-start(bf16[3,8,32,1024]{3,2,0,1:T(8,128)(2,1)} %copy.256), calls=%async_computation.1 | async-start | bytes 3145728 | tf_op jit(solution)/shard_map/all_to_all | solution.py:95
  23.2 91.3 %copy-start.39 = (pred[8,8]{0,1:T(8,128)(4,1)}, pred[8,8]{0,1:T(8,128)(4,1)S(1)}, u32[]{:S(2)}) copy-start(pred[8,8]{0,1:T(8,128)(4,1)S(1)} %copy.250) | copy-start | bytes 196
  26.2 39.5 %copy-start.6 = (bf16[1,1,512,1024]{2,3,1,0:T(8,128)(2,1)}, bf16[1,1,512,1024]{2,3,1,0:T(8,128)(2,1)S(1)}, u32[]{:S(2)}) copy-start(bf16[1,1,512,1024]{2,3,1,0:T(8,128)(2,1)S(1)} %copy.339) | copy-start | bytes 3145732
  60.9 42.6 %all-to-all-start = ((bf16[3,8,32,1024]{3,2,0,1:T(8,128)(2,1)}), bf16[3,8,32,1024]{3,2,0,1:T(8,128)(2,1)}, u32[]{:S(2)}, u32[]{:S(2)}) async-start(bf16[3,8,32,1024]{3,2,0,1:T(8,128)(2,1)} %copy.248), calls=%async_computation | async-start | bytes 3145728 | tf_op jit(solution)/shard_map/all_to_all | solution.py:95
  68.5 3.3 copy-start.2
  68.6 3.3 copy-start.14
  105.9 1.2 copy-start.10
  105.9 1.6 copy-start.12
  106.0 1.1 copy-start.21
  107.0 2.9 copy-start.4
  107.0 7.5 %copy-start.37 = (f32[32,8,8]{2,1,0:T(8,128)}, f32[32,8,8]{2,1,0:T(8,128)S(1)}, u32[]{:S(2)}) copy-start(f32[32,8,8]{2,1,0:T(8,128)S(1)} %get-tuple-element.40) | copy-start | bytes 24580
  107.5 2.5 copy-start.30
  109.5 1.2 copy-start.33
  122.6 30.8 %all-to-all-start.2 = ((bf16[8,2,32,1024]{3,2,1,0:T(8,128)(2,1)}), bf16[8,2,32,1024]{3,2,1,0:T(8,128)(2,1)}, u32[]{:S(2)}, u32[]{:S(2)}) async-start(bf16[8,2,32,1024]{3,2,1,0:T(8,128)(2,1)} %copy.262), calls=%async_computation.2 | async-start | bytes 2097152 | tf_op jit(solution)/shard_map/all_to_all | solution.py:119
  126.9 243.0 %reduce-scatter.2.cloned.1.call-start = ((), (), s32[]{:S(2)}) async-start(), calls=%async_computation.9 | async-start | bytes 8650752 | tf_op jit(solution)/shard_map/reduce_scatter | solution.py:134
  169.9 26.7 %all-to-all-start.5 = ((bf16[8,32,1024]{2,1,0:T(8,128)(2,1)}), bf16[8,32,1024]{2,1,0:T(8,128)(2,1)}, u32[]{:S(2)}, u32[]{:S(2)}) async-start(bf16[8,32,1024]{2,1,0:T(8,128)(2,1)} %get-tuple-element.36), calls=%async_computation.5 | async-start | bytes 1048576 | tf_op jit(solution)/shard_map/all_to_all | solution.py:139
  196.6 27.9 %all-to-all-start.3 = ((bf16[8,32,1024]{2,1,0:T(8,128)(2,1)}), bf16[8,32,1024]{2,1,0:T(8,128)(2,1)}, u32[]{:S(2)}, u32[]{:S(2)}) async-start(bf16[8,32,1024]{2,1,0:T(8,128)(2,1)} %get-tuple-element.37), calls=%async_computation.3 | async-start | bytes 1048576 | tf_op jit(solution)/shard_map/all_to_all | solution.py:139
  207.1 1.2 copy-start.17
  208.3 17.4 %copy-start.5 = (f32[32,8,8,8]{2,3,1,0:T(8,128)S(1)}, f32[32,8,8,8]{2,3,1,0:T(8,128)}, u32[]{:S(2)}) copy-start(f32[32,8,8,8]{2,3,1,0:T(8,128)} %copy-done.4) | copy-start | bytes 196612
  234.4 1.9 copy-start.31
  234.4 1.9 copy-start.34
  234.4 1.9 copy-start.40
  234.4 3.5 copy-start.13
  238.0 3.5 copy-start.11
  238.5 3.0 copy-start.9
  242.0 1.1 copy-start.32
  249.8 4.8 %copy-start.26 = (bf16[32,8,128,8]{2,3,1,0:T(8,128)(2,1)S(1)}, bf16[32,8,128,8]{2,3,1,0:T(8,128)(2,1)}, u32[]{:S(2)}) copy-start(bf16[32,8,128,8]{2,3,1,0:T(8,128)(2,1)} %copy-done.25) | copy-start | bytes 1572868
  249.8 61.3 %all-to-all-start.6 = ((bf16[8,3,1,32,1024]{4,3,1,2,0:T(8,128)(2,1)}), bf16[8,3,1,32,1024]{4,3,1,2,0:T(8,128)(2,1)}, u32[]{:S(2)}, u32[]{:S(2)}) async-start(bf16[8,3,1,32,1024]{4,3,1,2,0:T(8,128)(2,1)} %fusion.90), calls=%async_computation.6 | async-start | bytes 3145728 | tf_op jit(solution)/shard_map/all_to_all | solution.py:16
  254.4 1.0 copy-start.29
  254.4 1.0 copy-start.41
  254.5 1.8 copy-start.22
  256.4 1.0 copy-start.20
  257.9 1.1 copy-start.28
  262.5 54.8 %copy-start.15 = (bf16[1,1,512,1024]{2,3,1,0:T(8,128)(2,1)S(1)}, bf16[1,1,512,1024]{2,3,1,0:T(8,128)(2,1)}, u32[]{:S(2)}) copy-start(bf16[1,1,512,1024]{2,3,1,0:T(8,128)(2,1)} %copy.340) | copy-start | bytes 3145732
  262.5 54.8 %copy-start.16 = (bf16[512,8,128]{0,2,1:T(8,128)(2,1)S(1)}, bf16[512,8,128]{0,2,1:T(8,128)(2,1)}, u32[]{:S(2)}) copy-start(bf16[512,8,128]{0,2,1:T(8,128)(2,1)} %copy.302) | copy-start | bytes 3145732
  262.5 54.8 %copy-start.38 = (f32[8,512,1]{1,0,2:T(8,128)S(1)}, f32[8,512,1]{1,0,2:T(8,128)}, u32[]{:S(2)}) copy-start(f32[8,512,1]{1,0,2:T(8,128)} %add_bitcast_fusion) | copy-start | bytes 49156
  311.1 52.2 %all-to-all-start.4 = ((bf16[8,3,1,32,1024]{4,3,1,2,0:T(8,128)(2,1)}), bf16[8,3,1,32,1024]{4,3,1,2,0:T(8,128)(2,1)}, u32[]{:S(2)}, u32[]{:S(2)}) async-start(bf16[8,3,1,32,1024]{4,3,1,2,0:T(8,128)(2,1)} %fusion.98), calls=%async_computation.4 | async-start | bytes 3145728 | tf_op jit(solution)/shard_map/all_to_all | solution.py:16
  317.3 5.1 %copy-start.7 = (bf16[1,1,512,1024]{2,3,1,0:T(8,128)(2,1)S(1)}, bf16[1,1,512,1024]{2,3,1,0:T(8,128)(2,1)}, u32[]{:S(2)}) copy-start(bf16[1,1,512,1024]{2,3,1,0:T(8,128)(2,1)} %copy-done.6) | copy-start | bytes 3145732
  322.4 2.0 copy-start.3
  336.3 1.6 copy-start.35
  366.9 1.5 copy-start.18
  368.4 3.3 copy-start.1
  (5 other events, 4.1 us)
Sparse Core Ops, SparseCore 0:
  9.9 90.2 all-gather.1
  164.3 175.4 reduce-scatter.1
